TPU v7x, 128 devices: a whole 4x4x4 slice. The times are simulated.
128 devices in a mesh: seq: 32 (over x, z, core), tp: 4 (over y).
Axes of the slice: x: 4, y: 4, z: 4, core: 2. Of those that a mesh axis runs over, the one named last changes fastest.
Arguments:
- tokens: bfloat16 [8192, 2048], P('seq'), may hold values from -6 to 6
- norm_gain: float32 [2048], replicated, may hold values from 0.1 to 1.9
- qkv_weight: bfloat16 [2048, 4096], P(None, 'tp'), may hold values from -0.125 to 0.125
- conv_weight: float32 [4, 4096], P(None, 'tp'), may hold values from -3 to 3
- gate_down: bfloat16 [2048, 16], replicated, may hold values from -0.125 to 0.125
- gate_up: bfloat16 [16, 1024], P(None, 'tp'), may hold values from -6 to 6
- gate_bias: float32 [1024], P('tp'), may hold values from 0.3 to 8.5
- out_gate_weight: bfloat16 [2048, 2048], P(None, 'tp'), may hold values from -0.125 to 0.125
- head_gain: float32 [512], replicated, may hold values from 0.1 to 1.9
- out_weight: bfloat16 [2048, 2048], P('tp'), may hold values from -0.125 to 0.125
- final_gain: float32 [2048], replicated, may hold values from 0.1 to 1.9
- embedding: bfloat16 [32000, 2048], P(('seq', 'tp')), may hold values from -0.5 to 0.5
- lengths: int32 [8], replicated, may hold values from 1 to 4096, as said below
- packed_order: int32 [8], replicated, may hold values from 0 to 7, each once
Outputs:
- hidden: bfloat16 [8192, 2048], P('seq', 'tp')
- last_states: float32 [8, 4, 256, 512], P(None, 'tp')
- conv_edges: float32 [8, 3, 4096], P(None, None, 'tp')
- last_norms: float32 [8], replicated
- max_logits: float32 [8, 128], P(None, ('seq', 'tp'))
Inputs may be any that keep to these rules, and one draw needn't show every extreme that they name: Request r of the initial order has lengths[r] tokens; the lengths sum to 8192, the largest is 4096 and the smallest is 1 or 2. packed_order names every request once; the packed positions hold the tokens of request packed_order[0], then those of packed_order[1], and so on.
All inputs are finite; a program needn't handle non-finite values.
Results may differ from a plain program's by a relative error of at most 0.015.
Values may be sent and summed in bfloat16 or wider, within the bound.
No kernel may reach another device: no remote copies, remote signals or barrier semaphores. Data moves between devices by JAX's collectives and lax.ppermute only.
A program may use at most 128 MiB of HBM per device.

v0:
```python
from functools import partial
import jax
import jax.numpy as jnp
from jax import lax
from jax.sharding import PartitionSpec as P

DK = 256
DV = 512
KCONV = 4
BLOCK = 64
HIGHEST_PRECISION = lax.Precision.HIGHEST


def prefix(array, axis, combine, identity):
    peers, place = (lax.axis_size(axis), lax.axis_index(axis))
    everything = jax.tree.map(
        lambda part, kind: lax.all_gather(part.astype(kind), axis),
        array,
        (jnp.bfloat16, jnp.bfloat16),
    )
    start = jax.tree.map(
        lambda part, zero: jnp.broadcast_to(jnp.asarray(zero, part.dtype), part.shape),
        array,
        identity,
    )

    def hop(k, before):
        reached = k < place
        new = combine(
            before, jax.tree.map(lambda part, own: part[k].astype(own.dtype), everything, array)
        )
        return jax.tree.map(lambda a, b: jnp.where(reached, a, b), new, before)

    return lax.fori_loop(0, peers, hop, start)


def passed_along(array, axis, by):
    peers = lax.axis_size(axis)
    pairs = [(i, i + by) for i in range(peers) if 0 <= i + by < peers]
    return lax.ppermute(array, axis, pairs)


def segments(lengths, packed_order, positions):
    request_count = lengths.shape[0]
    select = (packed_order[:, None] == jnp.arange(request_count, dtype=jnp.int32)[None, :]).astype(
        jnp.int32
    )
    packed_len = jnp.sum(select * lengths[None, :], axis=1)
    end_points = jnp.cumsum(packed_len)
    starts = end_points - packed_len
    segment = jnp.sum((positions[:, None] >= starts[None, :]).astype(jnp.int32), axis=1) - 1
    last_index = jnp.sum(select * (end_points - 1)[:, None], axis=0)
    return (segment, last_index)


def causal_conv(padded, padded_segment, conv_weight, row_count):
    running = jnp.zeros((row_count, padded.shape[1]), jnp.float32)
    current = padded_segment[KCONV - 1 :]
    for offset in range(KCONV):
        window = padded[offset : offset + row_count]
        same_segment = (padded_segment[offset : offset + row_count] == current)[:, None]
        running = running + jnp.where(same_segment, window, 0.0) * conv_weight[offset]
    return running


def activate(convolved, head_count):
    shaped = convolved.reshape(convolved.shape[0], head_count, 2 * DK + DV)
    channel = jnp.arange(2 * DK + DV)
    return jnp.where(channel < 2 * DK, jax.nn.silu(shaped), shaped).astype(jnp.bfloat16)


def advance(carry_state, key_floats, values, cumulative, segment, segment_before):
    total_decay = cumulative[-1]
    same_tail = (segment == segment[-1])[:, None, None]
    scaled = jnp.where(same_tail, key_floats * jnp.exp(total_decay[None] - cumulative), 0.0).astype(
        jnp.bfloat16
    )
    added = jnp.einsum("jhc,jhv->hcv", scaled, values, preferred_element_type=jnp.float32)
    through = segment[-1] == segment_before
    return jnp.where(through, jnp.exp(total_decay)[:, :, None] * carry_state, 0.0) + added


def state_at_ends(
    end_states, carry_state, key_floats, values, cumulative, segment, segment_before, offset
):
    length = segment.shape[0]
    inside_block = (offset >= 0) & (offset < length)

    def add_ends(previous):
        end_row = jnp.clip(offset, 0, length - 1)
        end_decay = cumulative[end_row]
        end_segment = segment[end_row]
        indices = jnp.arange(length)
        allowed = (
            (indices[None, :] <= end_row[:, None]) & (segment[None, :] == end_segment[:, None])
        )[:, :, None, None]
        spread = jnp.where(allowed, end_decay[:, None] - cumulative[None], 0.0)
        weighted = jnp.where(allowed, key_floats[None] * jnp.exp(spread), 0.0).astype(jnp.bfloat16)
        within = jnp.einsum("rjhc,jhv->rhcv", weighted, values, preferred_element_type=jnp.float32)
        carried = (end_segment == segment_before)[:, None, None, None]
        reached = jnp.where(carried, jnp.exp(end_decay)[:, :, :, None] * carry_state[None], 0.0)
        return jnp.where(inside_block[:, None, None, None], within + reached, previous)

    def keep(previous):
        return previous

    return lax.cond(jnp.any(inside_block), add_ends, keep, end_states)


def block_step(last_index, carry, inputs):
    carry_state, end_states = carry
    queries, key_rows, values, decays, segment, segment_before, block_first = inputs
    cumulative = jnp.cumsum(decays, axis=0)
    length = segment.shape[0]
    indices = jnp.arange(length)
    causal = (indices[None, :] <= indices[:, None]) & (segment[None, :] == segment[:, None])
    allowed = causal[:, :, None, None]
    spread = jnp.where(allowed, cumulative[:, None] - cumulative[None, :], 0.0)
    weights = jnp.where(allowed, jnp.exp(spread), 0.0)
    query_rows = queries.astype(jnp.float32)
    key_floats = key_rows.astype(jnp.float32)
    scores = jnp.sum(query_rows[:, None] * key_floats[None, :] * weights, axis=-1).astype(
        jnp.bfloat16
    )
    inside = jnp.einsum("ijh,jhv->ihv", scores, values, preferred_element_type=jnp.float32)
    carried = (segment == segment_before)[:, None, None]
    outside = jnp.einsum(
        "ihc,hcv->ihv", query_rows * jnp.exp(cumulative), carry_state, precision=HIGHEST_PRECISION
    )
    output = inside + jnp.where(carried, outside, 0.0)
    new_state = advance(carry_state, key_floats, values, cumulative, segment, segment_before)
    end_states = state_at_ends(
        end_states,
        carry_state,
        key_floats,
        values,
        cumulative,
        segment,
        segment_before,
        last_index - block_first,
    )
    return ((new_state, end_states), output)


def state_only(carry_state, inputs):
    block_queries, block_keys, block_values, block_decays, block_segment, before, block_start = (
        inputs
    )
    cumulative = jnp.cumsum(block_decays, axis=0)
    return (
        advance(
            carry_state,
            block_keys.astype(jnp.float32),
            block_values,
            cumulative,
            block_segment,
            before,
        ),
        None,
    )


def head_output(attended, gate_out, head_gain):
    row_count, head_count, value_width = attended.shape
    mean_square = jnp.mean(attended * attended, axis=2, keepdims=True)
    gate_values = jax.nn.silu(
        gate_out.astype(jnp.float32).reshape(row_count, head_count, value_width)
    )
    gated = attended * lax.rsqrt(mean_square + 1e-05) * head_gain * gate_values
    return gated.reshape(row_count, head_count * value_width).astype(jnp.bfloat16)


def carry_in(decay_factor, local_state):

    def combine(earlier, later):
        return (earlier[0] * later[0], later[0][:, :, None] * earlier[1] + later[1])

    identity = (jnp.ones_like(decay_factor), jnp.zeros_like(local_state))
    result = prefix((decay_factor, local_state), "seq", combine, identity)
    return result[1]


def shards(
    tokens,
    norm_gain,
    qkv_weight,
    conv_weight,
    gate_down,
    gate_up,
    gate_bias,
    out_gate_weight,
    head_gain,
    out_weight,
    final_gain,
    embedding,
    lengths,
    packed_order,
):
    row_count = tokens.shape[0]
    head_count = out_weight.shape[0] // DV
    column_count = tokens.shape[1] // lax.axis_size("tp")
    start_row = lax.axis_index("seq") * row_count
    positions = start_row + jnp.arange(-(KCONV - 1), row_count, dtype=jnp.int32)
    segment_all, last_index = segments(lengths, packed_order, positions)
    segment = segment_all[KCONV - 1 :]
    segment_prior = segment_all[KCONV - 2]
    first_index = last_index - lengths + 1
    residual = tokens.astype(jnp.float32)
    normed = (
        residual
        * lax.rsqrt(jnp.mean(residual * residual, axis=1, keepdims=True) + 1e-06)
        * norm_gain
    ).astype(jnp.bfloat16)
    projected = jnp.dot(normed, qkv_weight, preferred_element_type=jnp.float32).astype(jnp.bfloat16)
    rim_rows = passed_along(projected[row_count - (KCONV - 1) :], "seq", 1)
    padded = jnp.concatenate([rim_rows, projected], axis=0)
    convolved = causal_conv(padded.astype(jnp.float32), segment_all, conv_weight, row_count)
    activated = activate(convolved, head_count)
    queries = activated[:, :, :DK]
    key_rows = activated[:, :, DK : 2 * DK]
    values = activated[:, :, 2 * DK :]
    lowrank = jnp.dot(normed, gate_down, preferred_element_type=jnp.float32)
    gate_logits = (
        jnp.dot(lowrank, gate_up.astype(jnp.float32), precision=HIGHEST_PRECISION) + gate_bias
    )
    decays = (jax.nn.log_sigmoid(gate_logits) / 16.0).reshape(row_count, head_count, DK)
    gate_out = jnp.dot(normed, out_gate_weight, preferred_element_type=jnp.float32).astype(
        jnp.bfloat16
    )
    block_count = row_count // BLOCK

    def split_blocks(array):
        return array.reshape((block_count, BLOCK) + array.shape[1:])

    segment_before = segment_all[KCONV - 2 : KCONV - 2 + row_count : BLOCK]
    block_first = start_row + jnp.arange(block_count, dtype=jnp.int32) * BLOCK
    block_inputs = (
        split_blocks(queries),
        split_blocks(key_rows),
        split_blocks(values),
        split_blocks(decays),
        split_blocks(segment),
        segment_before,
        block_first,
    )
    through_shard = segment[-1] == segment_prior
    empty_state = jnp.zeros((head_count, DK, DV), jnp.float32)
    empty_ends = jnp.zeros((lengths.shape[0], head_count, DK, DV), jnp.float32)
    stepper = partial(block_step, last_index)
    local_state, unused_steps = lax.scan(state_only, empty_state, block_inputs)
    decay_factor = jnp.where(through_shard, jnp.exp(jnp.sum(decays, axis=0)), 0.0)
    incoming = carry_in(decay_factor, local_state)
    (unused_state, end_states), attended = lax.scan(stepper, (incoming, empty_ends), block_inputs)
    attended = attended.reshape(row_count, head_count, DV)
    gated = head_output(attended, gate_out, head_gain)
    projected_out = jnp.dot(gated, out_weight, preferred_element_type=jnp.float32)
    summed = lax.psum_scatter(
        projected_out.astype(jnp.bfloat16), "tp", scatter_dimension=1, tiled=True
    ).astype(jnp.float32)
    column_start = lax.axis_index("tp") * column_count
    own_columns = lax.dynamic_slice_in_dim(residual, column_start, column_count, 1)
    hidden = (own_columns + summed).astype(jnp.bfloat16)
    owned_here = (last_index >= start_row) & (last_index < start_row + row_count)
    local_last = jnp.clip(last_index - start_row, 0, row_count - 1)
    last_rows = jnp.where(owned_here[:, None], hidden[local_last].astype(jnp.float32), 0.0)
    edge_list = []
    for offset in range(KCONV - 1):
        located = last_index - (KCONV - 2) + offset
        inside = owned_here & (located >= first_index)
        picked = padded[jnp.clip(located - start_row + KCONV - 1, 0, row_count + KCONV - 2)].astype(
            jnp.float32
        )
        edge_list.append(jnp.where(inside[:, None], picked, 0.0))
    conv_edges = jnp.stack(edge_list, axis=1)
    row_sums, conv_edges, last_states = (
        lax.psum(last_rows.astype(jnp.bfloat16), "seq").astype(jnp.float32),
        lax.psum(conv_edges.astype(jnp.bfloat16), "seq").astype(jnp.float32),
        lax.psum(end_states.astype(jnp.bfloat16), "seq").astype(jnp.float32),
    )
    full_rows = lax.all_gather(row_sums, "tp", axis=1, tiled=True)
    mean_square = jnp.mean(full_rows * full_rows, axis=1)
    last_norms = jnp.sqrt(mean_square)
    final_rows = (full_rows * lax.rsqrt(mean_square[:, None] + 1e-06) * final_gain).astype(
        jnp.bfloat16
    )
    logits = jnp.dot(final_rows, embedding.T, preferred_element_type=jnp.float32)
    max_logits = jnp.max(logits, axis=1, keepdims=True)
    return (hidden, last_states, conv_edges, last_norms, max_logits)


def solution(mesh):
    in_specs = (
        P("seq", None),
        P(),
        P(None, "tp"),
        P(None, "tp"),
        P(),
        P(None, "tp"),
        P("tp"),
        P(None, "tp"),
        P(),
        P("tp", None),
        P(),
        P(("seq", "tp"), None),
        P(),
        P(),
    )
    out_specs = (
        P("seq", "tp"),
        P(None, "tp", None, None),
        P(None, None, "tp"),
        P(),
        P(None, ("seq", "tp")),
    )
    return jax.shard_map(shards, mesh=mesh, in_specs=in_specs, out_specs=out_specs, check_vma=False)
```

profile of v0, /device:TPU:0, one launch (start us, length us, event | category | flops | bytes accessed | tf_op | source)
XLA Modules:
  0.0 477.1 jit_solution(16728195551736005816)
XLA Ops:
  7.2 1.6 multiply_reduce_fusion.1
  9.0 3.9 convolution_convert_fusion.1
  12.9 1.3 collective-permute-start
  14.8 1.7 fusion.70
  17.2 1.0 copy.52
  18.2 1.0 pad_maximum_fusion
  21.1 21.8 %while.43 = (s32[]{:T(128)}, f32[1,256,512]{2,1,0:T(8,128)S(1)}, s32[4,64]{1,0:T(4,128)S(1)}, s32[4]{0:T(128)S(1)}, f32[4,64,1,256]{3,2,1,0:T(1,128)}, /*index=5...) while((s32[]{:T(128)}, f32[1,256,512]{2,1,0:T(8,128)S(1)}, ...), condition=%wide.region_7.8_spmd.clone, body=%wide.region_5.7_spmd.clone.sunk | while | flops 18415684 | bytes 1417237 | solution.py:250
  25.3 1.2 fusion.123
  30.8 1.2 fusion.123
  36.2 1.2 fusion.123
  41.7 1.2 fusion.123
  45.5 26.3 %all-gather.2 = bf16[32,1,256]{2,1,0:T(2,128)(2,1)S(1)} all-gather(bf16[1,1,256]{2,1,0:T(2,128)(2,1)S(1)} %reshape.975), channel_id=2, replica_groups=mesh['seq'=32,'tp'=4] {'seq'}, dimensions={0}, use_global_device_ids=true | all-gather | bytes 16896 | tf_op jit(solution)/shard_map/all_gather | solution.py:17
  71.9 29.0 %all-gather.5.cloned.1.call-done = bf16[32,256,512]{2,1,0:T(8,128)(2,1)} async-done(((bf16[1,256,512]{2,1,0:T(8,128)(2,1)}), bf16[32,256,512]{2,1,0:T(8,128)(2,1)}) %all-gather.5.cloned.1.call-update) | async-done | bytes 8388624 | tf_op jit(solution)/shard_map/all_gather | solution.py:17
  101.0 36.2 %while.44 = (s32[]{:T(128)}, f32[1,256,512]{2,1,0:T(8,128)S(1)}, s32[]{:T(128)}, bf16[32,1,256]{2,1,0:T(2,128)(2,1)S(1)}, bf16[32,1,256,512]{3,2,1,0:T(8,128)(2,1)}, /*index=5*/s32[]{:T(128)}, s32[]{:T(128)}) while((s32[]{:T(128)}, f32[1,256,512]{2,1,0:T(8,128)S(1)}, s32[]{:T(128)}, bf16[32,1,256]{2,1,0:T(2,128)(2,1)S(1)}, ...), condition=%wide.region_9.10_spmd.clone, body=%wide.region_8.9_spmd.clone.sunk | while | flops 655620 | bytes 1313385 | solution.py:34
  101.0 1.1 fusion.124
  102.1 1.1 fusion.124
  103.2 1.1 fusion.124
  104.4 1.1 fusion.124
  105.5 1.1 fusion.124
  106.6 1.1 fusion.124
  107.7 1.1 fusion.124
  108.9 1.1 fusion.124
  110.0 1.1 fusion.124
  111.1 1.1 fusion.124
  112.3 1.1 fusion.124
  113.4 1.1 fusion.124
  114.5 1.1 fusion.124
  115.7 1.1 fusion.124
  116.8 1.1 fusion.124
  117.9 1.1 fusion.124
  119.1 1.1 fusion.124
  120.2 1.1 fusion.124
  121.3 1.1 fusion.124
  122.5 1.1 fusion.124
  123.6 1.1 fusion.124
  124.7 1.1 fusion.124
  125.9 1.1 fusion.124
  127.0 1.1 fusion.124
  128.1 1.1 fusion.124
  129.2 1.1 fusion.124
  130.4 1.1 fusion.124
  131.5 1.1 fusion.124
  132.6 1.1 fusion.124
  133.8 1.1 fusion.124
  134.9 1.1 fusion.124
  136.0 1.1 fusion.124
  137.1 1.5 broadcast_in_dim.240
  138.6 54.6 %while.42 = (s32[]{:T(128)}, f32[1,256,512]{2,1,0:T(8,128)S(1)}, bf16[8,1,256,512]{3,2,0,1:T(8,128)(2,1)}, f32[4,64,1,512]{3,1,2,0:T(8,128)}, s32[4,64]{1,0:T(4,...) while((s32[]{:T(128)}, f32[1,256,512]{2,1,0:T(8,128)S(1)}, ...), condition=%wide.region_17.18_spmd, body=%wide.region_11.17_spmd.sunk | while | flops 268659424 | bytes 8804605 | solution.py:253
  144.4 5.7 %conditional.2 = (bf16[8,1,256,512]{3,2,0,1:T(8,128)(2,1)}) conditional(s32[]{:T(128)} %convert_element_type.388, bf16[8,1,256,512]{3,2,0,1:T(8,128)(2,1)} %get-tuple-element.722, (pred[8]{0:T(512)(128)(4,1)S(1)}, s32[8]{0:T(128)S(1)}, s32[64]{0:T(128)S(1)}, bf16[1,64,1,256]{3,2,1,0:T(2,128)(2,1)S(1)}, f32[64,1,256]{2,1,0:T(1,128)S(1)}, ...), branch_computations={%region_14.14_spmd, %region_15.15_spmd} | conditional | flops 139086368 | bytes 5199492 | solution.py:107
  146.4 3.7 fusion
  150.3 2.0 multiply_reduce_fusion.5
  162.5 2.0 multiply_reduce_fusion.5
  174.7 2.0 multiply_reduce_fusion.5
  187.0 2.0 multiply_reduce_fusion.5
  194.5 2.8 fusion.56
  197.3 1.7 convolution_convert_fusion
  199.0 2.8 convert_element_type.287
  203.9 96.7 %all-reduce.3.cloned.1.call-done = bf16[8,1,256,512]{3,2,1,0:T(8,128)(2,1)} async-done(((bf16[8,1,256,512]{3,2,1,0:T(8,128)(2,1)}), bf16[8,1,256,512]{3,2,1,0:T(8,128)(2,1)}) %all-reduce.3.cloned.1.call-update) | async-done | bytes 2097168 | tf_op jit(solution)/shard_map/psum | solution.py:278
  300.6 4.2 convert_element_type.304
  304.8 21.7 %reduce-scatter.2.cloned.1.call-done = bf16[256,512]{1,0:T(8,128)(2,1)} async-done(((bf16[256,2048]{1,0:T(8,128)(2,1)}), bf16[256,512]{1,0:T(8,128)(2,1)}) %reduce-scatter.2.cloned.1.call-update) | async-done | bytes 262160 | tf_op jit(solution)/shard_map/reduce_scatter | solution.py:257
  326.5 1.2 add_convert_fusion
  328.3 126.8 %all-reduce = (bf16[8,3,1024]{2,0,1:T(8,128)(2,1)S(1)}, bf16[8,512]{1,0:T(8,128)(2,1)S(1)}) all-reduce(bf16[8,3,1024]{2,0,1:T(8,128)(2,1)S(1)} %pad_maximum_fusion.1, bf16[8,512]{1,0:T(8,128)(2,1)S(1)} %select_convert_fusion.2), channel_id=1, replica_groups=mesh['seq'=32,'tp'=4] {'seq'}, use_global_device_ids=true, to_apply=%region_21.22 | all-reduce | flops 28672 | bytes 114688 | tf_op jit(solution)/shard_map/psum | solution.py:277
  455.2 11.9 %all_gather.16 = f32[8,2048]{1,0:T(8,128)S(1)} all-gather(f32[8,512]{1,0:T(8,128)S(1)} %convert_element_type.314), channel_id=1, replica_groups=mesh['seq'=32,'tp'=4] {'tp'}, dimensions={1}, use_global_device_ids=true | all-gather | bytes 81920 | tf_op jit(solution)/shard_map/all_gather | solution.py:280
  468.3 2.2 convolution_reduce_fusion
  (243 shorter events, 56.2 us)
Async XLA Ops:
  7.2 190.1 %copy-start = (bf16[512,2048]{1,0:T(8,128)(2,1)S(1)}, bf16[512,2048]{1,0:T(8,128)(2,1)}, u32[]{:S(2)}) copy-start(bf16[512,2048]{1,0:T(8,128)(2,1)} %param.31) | copy-start | bytes 6291460
  7.2 93.8 %all-gather.5.cloned.1.call-start = ((), (), s32[]{:S(2)}) async-start(), calls=%async_computation.3 | async-start | bytes 8650752 | tf_op jit(solution)/shard_map/all_gather | solution.py:17
  8.9 5.3 %copy-start.6 = (s32[8]{0:T(128)S(1)}, s32[8]{0:T(128)}, u32[]{:S(2)}) copy-start(s32[8]{0:T(128)} %param.34) | copy-start | bytes 100
  8.9 5.3 %copy-start.12 = (s32[8]{0:T(128)S(1)}, s32[8]{0:T(128)}, u32[]{:S(2)}) copy-start(s32[8]{0:T(128)} %param.35) | copy-start | bytes 100
  8.9 5.8 %copy-start.4 = (f32[4,1024]{1,0:T(4,128)S(1)}, f32[4,1024]{1,0:T(4,128)}, u32[]{:S(2)}) copy-start(f32[4,1024]{1,0:T(4,128)} %param.25) | copy-start | bytes 49156
  8.9 5.8 %copy-start.7 = (bf16[2048,16]{0,1:T(8,128)(2,1)S(1)}, bf16[2048,16]{0,1:T(8,128)(2,1)}, u32[]{:S(2)}) copy-start(bf16[2048,16]{0,1:T(8,128)(2,1)} %param.26) | copy-start | bytes 196612
  8.9 5.8 %copy-start.9 = (f32[2048]{0:T(1024)S(1)}, f32[2048]{0:T(1024)}, u32[]{:S(2)}) copy-start(f32[2048]{0:T(1024)} %param.23) | copy-start | bytes 24580
  8.9 7.5 %copy-start.8 = (bf16[16,256]{1,0:T(8,128)(2,1)S(1)}, bf16[16,256]{1,0:T(8,128)(2,1)}, u32[]{:S(2)}) copy-start(bf16[16,256]{1,0:T(8,128)(2,1)} %param.27) | copy-start | bytes 24580
  9.0 7.5 %copy-start.11 = (f32[256]{0:T(256)S(1)}, f32[256]{0:T(256)}, u32[]{:S(2)}) copy-start(f32[256]{0:T(256)} %param.28) | copy-start | bytes 3076
  12.9 5.3 %collective-permute-start = (bf16[3,1024]{1,0:T(4,128)(2,1)S(1)}, bf16[3,1024]{1,0:T(4,128)(2,1)S(1)}, u32[]{:S(2)}, u32[]{:S(2)}) collective-permute-start(bf16[3,1024]{1,0:T(4,128)(2,1)S(1)} %slice.111), channel_id=1, source_target_pairs={{0,4},{4,8},{8,12},{12,16},{16,20},{20,24},{24,28},{28,32},{32,36}... | collective-permute-start | bytes 18440 | tf_op jit(solution)/shard_map/ppermute | solution.py:40
  43.6 257.0 %all-reduce.3.cloned.1.call-start = ((), (), s32[]{:S(2)}) async-start(), calls=%async_computation.2 | async-start | bytes 4194304 | tf_op jit(solution)/shard_map/psum | solution.py:278
  193.3 1.0 copy-start.2
  193.3 1.2 copy-start.10
  193.3 133.2 %reduce-scatter.2.cloned.1.call-start = ((), (), s32[]{:S(2)}) async-start(), calls=%async_computation.1 | async-start | bytes 1310720 | tf_op jit(solution)/shard_map/reduce_scatter | solution.py:257
  199.0 2.9 copy-start.1
  203.9 264.4 %copy-start.5 = (f32[2048]{0:T(1024)S(1)}, f32[2048]{0:T(1024)}, u32[]{:S(2)}) copy-start(f32[2048]{0:T(1024)} %param.32) | copy-start | bytes 24580
  327.7 142.9 %copy-start.3 = (bf16[256,512]{1,0:T(8,128)(2,1)}, bf16[256,512]{1,0:T(8,128)(2,1)S(1)}, u32[]{:S(2)}) copy-start(bf16[256,512]{1,0:T(8,128)(2,1)S(1)} %add_convert_fusion) | copy-start | bytes 786436
Sparse Core Ops, SparseCore 0:
  43.7 57.1 all-gather.4
  193.4 107.1 all-reduce.2
  303.0 23.4 reduce-scatter.1
where the time goes:
time: 480 us; the launch traced here: 477 us
  blocking collectives  165 us (34%)
  waiting for transfers between devices  147 us (31%)
  other arithmetic  81.7 us (17%)
  matrix products  27.2 us (6%)
  local copies, waits for them, and re-layouts  24.3 us (5%)
  between operations  15.3 us (3%)
  loops' own time  14.8 us (3%)
    psum x1, blocking collectives, shards(): lax.psum(conv_edges.astype(jnp.bfloat16), 'seq').astype(jnp.float32)  127 us
    psum x1, waiting for transfers between devices, shards(): lax.psum(end_states.astype(jnp.bfloat16), 'seq').astype(jnp.float32)  96.7 us
    select_n x32, other arithmetic, hop(): return jax.tree.map(lambda a, b: jnp.where(reached, a, b), new, before)  34.9 us
    all_gather x1, waiting for transfers between devices, prefix(): lax.all_gather(part.astype(kind), axis)  29 us
    all_gather x1, blocking collectives, prefix(): lax.all_gather(part.astype(kind), axis)  26.3 us
    reduce_scatter x1, waiting for transfers between devices, shards(): lax.psum_scatter(projected_out.astype(jnp.bfloat16), 'tp', scatter_dimens...  21.7 us
    all_gather x1, blocking collectives, shards(): full_rows = lax.all_gather(row_sums, 'tp', axis=1, tiled=True)  11.9 us
    dynamic_slice x24, local copies, waits for them, and re-layouts, shards(): local_state, unused_steps = lax.scan(state_only, empty_state, block_inputs)  10.5 us
  transfers between devices with their start and end apart: 4, of which 3 were waited for; matrix products, arithmetic and copies ran while one was open for 4% of the time, Pallas kernels for 0%

commit v1 on v0

--- a/solution.py
+++ b/solution.py
@@ -274,7 +274,7 @@
     conv_edges = jnp.stack(edge_list, axis=1)
     row_sums, conv_edges, last_states = (
         lax.psum(last_rows.astype(jnp.bfloat16), "seq").astype(jnp.float32),
-        lax.psum(conv_edges.astype(jnp.bfloat16), "seq").astype(jnp.float32),
+        jnp.sum(lax.all_gather(conv_edges.astype(jnp.bfloat16), "seq"), axis=0).astype(jnp.float32),
         lax.psum(end_states.astype(jnp.bfloat16), "seq").astype(jnp.float32),
     )
     full_rows = lax.all_gather(row_sums, "tp", axis=1, tiled=True)

time: 480 us -> 421 us (0.88)
  blocking collectives: 165 us -> 106 us
    psum x1, blocking collectives: 127 us -> 66.8 us  [shards(): lax.psum(last_rows.astype(jnp.bfloat16), 'seq').astype(jnp.float32)]
  transfers between devices with their start and end apart: 4 -> 5, of which waited for: 3 -> 3; matrix products, arithmetic and copies ran while one was open for 4% -> 25% of each run, Pallas kernels for 0% -> 0%
where the time goes in v1:
time: 421 us; the launch traced here: 418 us
  waiting for transfers between devices  144 us (34%)
  blocking collectives  106 us (25%)
  other arithmetic  84.4 us (20%)
  local copies, waits for them, and re-layouts  28 us (7%)
  matrix products  24.5 us (6%)
  between operations  15.4 us (4%)
  loops' own time  14.5 us (3%)
    psum x1, waiting for transfers between devices, shards(): lax.psum(end_states.astype(jnp.bfloat16), 'seq').astype(jnp.float32)  97.6 us
    psum x1, blocking collectives, shards(): lax.psum(last_rows.astype(jnp.bfloat16), 'seq').astype(jnp.float32)  66.8 us
    select_n x32, other arithmetic, hop(): return jax.tree.map(lambda a, b: jnp.where(reached, a, b), new, before)  34.9 us
    all_gather x1, blocking collectives, prefix(): lax.all_gather(part.astype(kind), axis)  27 us
    all_gather x1, waiting for transfers between devices, prefix(): lax.all_gather(part.astype(kind), axis)  25.1 us
    reduce_scatter x1, waiting for transfers between devices, shards(): lax.psum_scatter(projected_out.astype(jnp.bfloat16), 'tp', scatter_dimens...  21.6 us
    dynamic_slice x24, local copies, waits for them, and re-layouts, shards(): local_state, unused_steps = lax.scan(state_only, empty_state, block_inputs)  13.7 us
    all_gather x1, blocking collectives, shards(): full_rows = lax.all_gather(row_sums, 'tp', axis=1, tiled=True)  11.9 us
  transfers between devices with their start and end apart: 5, of which 3 were waited for; matrix products, arithmetic and copies ran while one was open for 25% of the time, Pallas kernels for 0%

profile of v1, /device:TPU:0, one launch (start us, length us, event | category | flops | bytes accessed | tf_op | source)
XLA Modules:
  0.0 418.2 jit_solution(17041458056240697764)
XLA Ops:
  7.2 1.6 multiply_reduce_fusion.1
  9.0 3.9 convolution_convert_fusion.1
  13.7 1.3 collective-permute-start
  17.8 1.2 pad_maximum_fusion
  21.5 21.8 %while.43 = (s32[]{:T(128)}, f32[1,256,512]{2,1,0:T(8,128)S(1)}, s32[4,64]{1,0:T(4,128)S(1)}, s32[4]{0:T(128)S(1)}, f32[4,64,1,256]{3,2,1,0:T(1,128)}, /*index=5...) while((s32[]{:T(128)}, f32[1,256,512]{2,1,0:T(8,128)S(1)}, ...), condition=%wide.region_7.8_spmd.clone, body=%wide.region_5.7_spmd.clone.sunk | while | flops 18415684 | bytes 1417237 | solution.py:250
  25.8 1.2 fusion.126
  31.2 1.2 fusion.126
  36.7 1.2 fusion.126
  42.1 1.2 fusion.126
  46.0 27.0 %all-gather.2 = bf16[32,1,256]{2,1,0:T(2,128)(2,1)S(1)} all-gather(bf16[1,1,256]{2,1,0:T(2,128)(2,1)S(1)} %reshape.1038), channel_id=2, replica_groups=mesh['seq'=32,'tp'=4] {'seq'}, dimensions={0}, use_global_device_ids=true | all-gather | bytes 16896 | tf_op jit(solution)/shard_map/all_gather | solution.py:17
  76.3 25.1 %all-gather.8.cloned.1.call-done = bf16[32,256,512]{2,1,0:T(8,128)(2,1)} async-done(((bf16[1,256,512]{2,1,0:T(8,128)(2,1)}), bf16[32,256,512]{2,1,0:T(8,128)(2,1)}) %all-gather.8.cloned.1.call-update) | async-done | bytes 8388624 | tf_op jit(solution)/shard_map/all_gather | solution.py:17
  101.4 36.2 %while.44 = (s32[]{:T(128)}, f32[1,256,512]{2,1,0:T(8,128)S(1)}, s32[]{:T(128)}, bf16[32,1,256]{2,1,0:T(2,128)(2,1)S(1)}, bf16[32,1,256,512]{3,2,1,0:T(8,128)(2,1)}, /*index=5*/s32[]{:T(128)}, s32[]{:T(128)}) while((s32[]{:T(128)}, f32[1,256,512]{2,1,0:T(8,128)S(1)}, s32[]{:T(128)}, bf16[32,1,256]{2,1,0:T(2,128)(2,1)S(1)}, ...), condition=%wide.region_9.10_spmd.clone, body=%wide.region_8.9_spmd.clone.sunk | while | flops 655620 | bytes 1313385 | solution.py:34
  101.4 1.1 fusion.127
  102.5 1.1 fusion.127
  103.7 1.1 fusion.127
  104.8 1.1 fusion.127
  105.9 1.1 fusion.127
  107.1 1.1 fusion.127
  108.2 1.1 fusion.127
  109.3 1.1 fusion.127
  110.5 1.1 fusion.127
  111.6 1.1 fusion.127
  112.7 1.1 fusion.127
  113.9 1.1 fusion.127
  115.0 1.1 fusion.127
  116.1 1.1 fusion.127
  117.3 1.1 fusion.127
  118.4 1.1 fusion.127
  119.5 1.1 fusion.127
  120.7 1.1 fusion.127
  121.8 1.1 fusion.127
  122.9 1.1 fusion.127
  124.1 1.1 fusion.127
  125.2 1.1 fusion.127
  126.3 1.1 fusion.127
  127.5 1.1 fusion.127
  128.6 1.1 fusion.127
  129.7 1.1 fusion.127
  130.8 1.1 fusion.127
  132.0 1.1 fusion.127
  133.1 1.1 fusion.127
  134.2 1.1 fusion.127
  135.4 1.1 fusion.127
  136.5 1.1 fusion.127
  137.6 1.5 broadcast_in_dim.240
  139.1 57.3 %while.42 = (s32[]{:T(128)}, f32[1,256,512]{2,1,0:T(8,128)S(1)}, bf16[8,1,256,512]{3,2,0,1:T(8,128)(2,1)}, f32[4,64,1,512]{3,1,2,0:T(8,128)}, s32[4,64]{1,0:T(4,...) while((s32[]{:T(128)}, f32[1,256,512]{2,1,0:T(8,128)S(1)}, ...), condition=%wide.region_17.18_spmd, body=%wide.region_11.17_spmd.sunk | while | flops 268659424 | bytes 8804605 | solution.py:253
  145.6 5.7 %conditional.2 = (bf16[8,1,256,512]{3,2,0,1:T(8,128)(2,1)}) conditional(s32[]{:T(128)} %convert_element_type.415, bf16[8,1,256,512]{3,2,0,1:T(8,128)(2,1)} %get-tuple-element.720, (pred[8]{0:T(512)(128)(4,1)S(1)}, s32[8]{0:T(128)S(1)}, s32[64]{0:T(128)S(1)}, bf16[1,64,1,256]{3,2,1,0:T(2,128)(2,1)S(1)}, f32[64,1,256]{2,1,0:T(1,128)S(1)}, ...), branch_computations={%region_14.14_spmd, %region_15.15_spmd} | conditional | flops 139086368 | bytes 5199492 | solution.py:107
  147.6 3.7 fusion
  151.5 2.0 multiply_reduce_fusion.5
  164.4 2.0 multiply_reduce_fusion.5
  177.3 2.0 multiply_reduce_fusion.5
  190.2 2.0 multiply_reduce_fusion.5
  196.5 1.2 multiply_reduce_fusion.2
  197.9 2.5 fusion.56
  200.4 1.7 convolution_convert_fusion
  202.2 1.5 convert_element_type.314
  203.7 1.7 reduce_sum.90
  206.1 97.6 %all-reduce.2.cloned.1.call-done = bf16[8,1,256,512]{3,2,1,0:T(8,128)(2,1)} async-done(((bf16[8,1,256,512]{3,2,1,0:T(8,128)(2,1)}), bf16[8,1,256,512]{3,2,1,0:T(8,128)(2,1)}) %all-reduce.2.cloned.1.call-update) | async-done | bytes 2097168 | tf_op jit(solution)/shard_map/psum | solution.py:278
  303.8 4.2 convert_element_type.331
  307.9 21.6 %reduce-scatter.2.cloned.1.call-done = bf16[256,512]{1,0:T(8,128)(2,1)} async-done(((bf16[256,2048]{1,0:T(8,128)(2,1)}), bf16[256,512]{1,0:T(8,128)(2,1)}) %reduce-scatter.2.cloned.1.call-update) | async-done | bytes 262160 | tf_op jit(solution)/shard_map/reduce_scatter | solution.py:257
  329.5 1.2 add_convert_fusion
  331.4 66.8 %psum.15 = bf16[8,512]{1,0:T(8,128)(2,1)S(1)} all-reduce(bf16[8,512]{1,0:T(8,128)(2,1)S(1)} %select_convert_fusion.2), channel_id=1, replica_groups=mesh['seq'=32,'tp'=4] {'seq'}, use_global_device_ids=true, to_apply=%region_22.23 | all-reduce | flops 4096 | bytes 16384 | tf_op jit(solution)/shard_map/psum | solution.py:276
  398.1 11.9 %all_gather.21 = f32[8,2048]{1,0:T(8,128)S(1)} all-gather(f32[8,512]{1,0:T(8,128)S(1)} %convert_element_type.341), channel_id=1, replica_groups=mesh['seq'=32,'tp'=4] {'tp'}, dimensions={1}, use_global_device_ids=true | all-gather | bytes 81920 | tf_op jit(solution)/shard_map/all_gather | solution.py:280
  410.7 1.0 convolution_reduce_fusion
  (257 shorter events, 62.2 us)
Async XLA Ops:
  7.2 193.2 %copy-start = (bf16[512,2048]{1,0:T(8,128)(2,1)S(1)}, bf16[512,2048]{1,0:T(8,128)(2,1)}, u32[]{:S(2)}) copy-start(bf16[512,2048]{1,0:T(8,128)(2,1)} %param.31) | copy-start | bytes 6291460
  7.2 94.2 %all-gather.8.cloned.1.call-start = ((), (), s32[]{:S(2)}) async-start(), calls=%async_computation.4 | async-start | bytes 8650752 | tf_op jit(solution)/shard_map/all_gather | solution.py:17
  8.9 6.1 %copy-start.8 = (s32[8]{0:T(128)S(1)}, s32[8]{0:T(128)}, u32[]{:S(2)}) copy-start(s32[8]{0:T(128)} %param.34) | copy-start | bytes 100
  8.9 6.1 %copy-start.14 = (s32[8]{0:T(128)S(1)}, s32[8]{0:T(128)}, u32[]{:S(2)}) copy-start(s32[8]{0:T(128)} %param.35) | copy-start | bytes 100
  8.9 6.7 %copy-start.6 = (f32[4,1024]{1,0:T(4,128)S(1)}, f32[4,1024]{1,0:T(4,128)}, u32[]{:S(2)}) copy-start(f32[4,1024]{1,0:T(4,128)} %param.25) | copy-start | bytes 49156
  8.9 6.7 %copy-start.1 = (bf16[256,2048]{1,0:T(8,128)(2,1)S(1)}, bf16[256,2048]{1,0:T(8,128)(2,1)}, u32[]{:S(2)}) copy-start(bf16[256,2048]{1,0:T(8,128)(2,1)} %param.22) | copy-start | bytes 3145732
  8.9 6.7 %copy-start.9 = (bf16[2048,16]{0,1:T(8,128)(2,1)S(1)}, bf16[2048,16]{0,1:T(8,128)(2,1)}, u32[]{:S(2)}) copy-start(bf16[2048,16]{0,1:T(8,128)(2,1)} %param.26) | copy-start | bytes 196612
  8.9 6.7 %copy-start.11 = (f32[2048]{0:T(1024)S(1)}, f32[2048]{0:T(1024)}, u32[]{:S(2)}) copy-start(f32[2048]{0:T(1024)} %param.23) | copy-start | bytes 24580
  9.0 7.1 %copy-start.10 = (bf16[16,256]{1,0:T(8,128)(2,1)S(1)}, bf16[16,256]{1,0:T(8,128)(2,1)}, u32[]{:S(2)}) copy-start(bf16[16,256]{1,0:T(8,128)(2,1)} %param.27) | copy-start | bytes 24580
  9.0 7.1 %copy-start.13 = (f32[256]{0:T(256)S(1)}, f32[256]{0:T(256)}, u32[]{:S(2)}) copy-start(f32[256]{0:T(256)} %param.28) | copy-start | bytes 3076
  12.9 0.8 copy-start.4
  13.7 4.1 collective-permute-start
  43.3 30.3 %copy-start.15 = (s32[4]{0:T(128)}, s32[4]{0:T(128)S(1)}, u32[]{:S(2)}) copy-start(s32[4]{0:T(128)S(1)} %get-tuple-element.765) | copy-start | bytes 52
  44.1 159.6 %all-gather.6.cloned.1.call-start = ((), (), s32[]{:S(2)}) async-start(), calls=%async_computation.3 | async-start | bytes 1622016 | tf_op jit(solution)/shard_map/all_gather | solution.py:277
  76.3 227.5 %all-reduce.2.cloned.1.call-start = ((), (), s32[]{:S(2)}) async-start(), calls=%async_computation.2 | async-start | bytes 4194304 | tf_op jit(solution)/shard_map/psum | solution.py:278
  137.6 1.5 copy-start.16
  137.6 1.5 copy-start.17
  196.4 1.4 copy-start.2
  196.5 1.4 copy-start.12
  196.5 133.0 %reduce-scatter.2.cloned.1.call-start = ((), (), s32[]{:S(2)}) async-start(), calls=%async_computation.1 | async-start | bytes 1310720 | tf_op jit(solution)/shard_map/reduce_scatter | solution.py:257
  206.1 204.5 %copy-start.3 = (bf16[250,2048]{1,0:T(8,128)(2,1)S(1)}, bf16[250,2048]{1,0:T(8,128)(2,1)}, u32[]{:S(2)}) copy-start(bf16[250,2048]{1,0:T(8,128)(2,1)} %param.33) | copy-start | bytes 3072004
  206.1 204.5 %copy-start.7 = (f32[2048]{0:T(1024)S(1)}, f32[2048]{0:T(1024)}, u32[]{:S(2)}) copy-start(f32[2048]{0:T(1024)} %param.32) | copy-start | bytes 24580
  330.7 81.0 %copy-start.5 = (bf16[256,512]{1,0:T(8,128)(2,1)}, bf16[256,512]{1,0:T(8,128)(2,1)S(1)}, u32[]{:S(2)}) copy-start(bf16[256,512]{1,0:T(8,128)(2,1)S(1)} %add_convert_fusion) | copy-start | bytes 786436
Sparse Core Ops, SparseCore 0:
  44.2 57.1 all-gather.7
  104.2 42.5 all-gather.5
  196.6 107.0 all-reduce.1
  306.0 23.4 reduce-scatter.1
